TPU v7x, 512 devices: a whole 4x4x16 slice. The times are simulated.
512 devices in a mesh: bond: 32 (over z, core), row: 16 (over y, x).
Axes of the slice: x: 4, y: 4, z: 16, core: 2. Of those that a mesh axis runs over, the one named last changes fastest.
Arguments:
- left_core: float32 [32, 384, 2, 384], P('bond', 'row'), may hold values from -1 to 2
- right_core: float32 [32, 384, 2, 384], P('bond', 'row'), may hold values from -1 to 2
- gate_angles: float32 [32, 6], P('bond'), may hold values from -3.140625 to 3.140625
- sketch: float32 [768, 384], P('bond'), may hold values from -0.21875 to 0.21875
Outputs:
- next_pair: float32 [32, 768, 768], P('bond', 'row')
All inputs are finite; a program needn't handle non-finite values.
Results may differ from a plain program's by a relative error of at most 0.0003.
Values sent between devices are 32-bit elements; how exact they have to be, the bound alone decides.
No kernel may reach another device: no remote copies, remote signals or barrier semaphores. Data moves between devices by JAX's collectives and lax.ppermute only.
A program may use at most 64 MiB of HBM per device.

v0:
```python
import jax
import jax.numpy as jnp
import numpy as np
from jax import lax
from jax.sharding import PartitionSpec as P

ITERS = 2
HIGHEST = lax.Precision.HIGHEST
PLANES = ((0, 1), (2, 3), (0, 2), (1, 3), (0, 3), (1, 2))


def from_behind(value, axis, steps):
    count = lax.axis_size(axis)
    initial, last = (max(0, -steps), min(count, count - steps))
    return lax.ppermute(value, axis, [(source, source + steps) for source in range(initial, last)])


def rotation(first_axis, second_axis, cosine, sine_value):
    unit = np.eye(4, dtype=np.float32)
    diag_part = np.outer(unit[first_axis], unit[first_axis]) + np.outer(
        unit[second_axis], unit[second_axis]
    )
    skew_part = np.outer(unit[second_axis], unit[first_axis]) - np.outer(
        unit[first_axis], unit[second_axis]
    )
    rest_part = np.eye(4, dtype=np.float32) - diag_part
    return (
        jnp.asarray(rest_part)
        + cosine * jnp.asarray(diag_part)
        + sine_value * jnp.asarray(skew_part)
    )


def build_gate(angles):
    gate_matrix = jnp.eye(4, dtype=jnp.float32)
    for number, plane in enumerate(PLANES):
        rotated = rotation(plane[0], plane[1], jnp.cos(angles[number]), jnp.sin(angles[number]))
        gate_matrix = jnp.dot(
            rotated, gate_matrix, precision=HIGHEST, preferred_element_type=jnp.float32
        )
    return gate_matrix


def apply_gate(two_site, gate_matrix):
    width = two_site.shape[1] // 2
    blocks = two_site.reshape(two_site.shape[0] // 2, 2, 2, width)
    mixed_gate = jnp.einsum(
        "pqtu,atuc->apqc", gate_matrix.reshape(2, 2, 2, 2), blocks, precision=HIGHEST
    )
    return mixed_gate.reshape(two_site.shape)


def matmul(left_side, right_side):
    return jnp.dot(left_side, right_side, precision=HIGHEST, preferred_element_type=jnp.float32)


def inner_rows(left_side, right_side):
    return lax.dot_general(
        left_side,
        right_side,
        (((0,), (0,)), ((), ())),
        precision=HIGHEST,
        preferred_element_type=jnp.float32,
    )


def orthonormal(sketched):
    gram_matrix = inner_rows(sketched, sketched)
    chol_factor = jnp.linalg.cholesky(gram_matrix)
    return lax.linalg.triangular_solve(
        chol_factor, sketched, left_side=False, lower=True, transpose_a=True
    )


def on_device(left_core, right_core, gate_angles, sketch):
    width = left_core.shape[3]
    local_sites = left_core.shape[1]
    local_rows = 2 * local_sites
    both = jnp.stack([left_core[0], right_core[0]], axis=1)
    both = lax.all_gather(both, "row", axis=0, tiled=True)
    sites = both.shape[0]
    left_matrix = both[:, 0].reshape(2 * sites, width)
    right_matrix = both[:, 1].reshape(sites, 2 * width)
    two_site = matmul(left_matrix, right_matrix)
    two_site = apply_gate(two_site, build_gate(gate_angles[0]))
    full_sketch = lax.all_gather(sketch, "bond", axis=0, tiled=True)
    ortho_basis = orthonormal(matmul(two_site, full_sketch))
    for repeat in range(ITERS):
        projected = inner_rows(two_site, ortho_basis)
        ortho_basis = orthonormal(matmul(two_site, projected))
    start = lax.axis_index("row") * local_sites
    my_columns = lax.dynamic_slice_in_dim(ortho_basis, start, local_sites, axis=1)
    carried = inner_rows(my_columns, two_site)
    incoming = from_behind(carried, "bond", 1)
    incoming_matrix = incoming.reshape(local_rows, width)
    next_block = matmul(incoming_matrix, ortho_basis.reshape(sites, 2 * width))
    return next_block[None]


def solution(mesh):
    return jax.shard_map(
        on_device,
        mesh=mesh,
        in_specs=(
            P("bond", "row", None, None),
            P("bond", "row", None, None),
            P("bond", None),
            P("bond", None),
        ),
        out_specs=P("bond", "row", None),
        check_vma=False,
    )
```

profile of v0, /device:TPU:1, one launch (start us, length us, event | category | flops | bytes accessed | tf_op | source)
XLA Modules:
  0.0 618.9 jit_solution(4283182410846225504)
XLA Ops:
  23.8 51.3 %all-gather.3.cloned.1.call-done = f32[384,2,2,384]{3,2,0,1:T(2,128)} async-done(((f32[24,2,2,384]{3,2,0,1:T(2,128)}), f32[384,2,2,384]{3,2,0,1:T(2,128)}) %all-gather.3.cloned.1.call-update) | async-done | bytes 2359312 | tf_op jit(solution)/shard_map/all_gather | solution.py:80
  75.1 2.4 slice_bitcast_fusion
  78.3 4.1 convolution_bitcast_fusion
  82.4 10.3 %fusion = f32[384,384,2,2,1]{1,3,4,2,0:T(2,128)S(1)} fusion(f32[384,2,2,384,1]{3,0,2,1,4:T(8,128)S(1)} %convolution_bitcast_fusion, f32[2,2,2,2]{3,2,1,0:T(2,128)S(1)} %reshape.66), kind=kOutput, calls=%fused_computation.6 | convolution fusion | flops 28311552 | bytes 4718656 | tf_op jit(solution)/shard_map/pqtu,atuc->apqc/dot_general | solution.py:47
  92.9 56.2 %all-gather.5.cloned.1.call-done = f32[768,384]{1,0:T(8,128)} async-done(((f32[24,384]{1,0:T(8,128)}), f32[768,384]{1,0:T(8,128)}) %all-gather.5.cloned.1.call-update) | async-done | bytes 1179664 | tf_op jit(solution)/shard_map/all_gather | solution.py:86
  149.2 5.1 fusion.123
  154.3 2.9 fusion.124
  157.1 2.1 copy.28
  162.0 13.2 %cholesky.273 = f32[128,128]{1,0:T(8,128)} custom-call(f32[128,128]{1,0:T(8,128)} %cholesky.428), custom_call_target="Cholesky" | custom-call | tf_op jit(solution)/shard_map/jit(cholesky)/cholesky | solution.py:69
  178.3 20.6 %custom-call.23 = f32[1,128,128]{1,2,0:T(8,128)} custom-call(f32[1,128,128]{2,1,0:T(8,128)} %get-tuple-element.82), custom_call_target="InvertDiagBlocksLowerTriangular" | custom-call | tf_op jit(solution)/shard_map/jit(cholesky)/cholesky | solution.py:69
  203.3 13.2 %cholesky.292 = f32[128,128]{1,0:T(8,128)} custom-call(f32[128,128]{1,0:T(8,128)} %cholesky.432), custom_call_target="Cholesky" | custom-call | tf_op jit(solution)/shard_map/jit(cholesky)/cholesky | solution.py:69
  217.9 11.3 %custom-call.24 = f32[1,128,128]{1,2,0:T(8,128)} custom-call(f32[1,128,128]{2,1,0:T(8,128)} %get-tuple-element.79), custom_call_target="InvertDiagBlocksLowerTriangular" | custom-call | tf_op jit(solution)/shard_map/jit(cholesky)/cholesky | solution.py:69
  232.8 13.2 %cholesky.311 = f32[128,128]{1,0:T(8,128)} custom-call(f32[128,128]{1,0:T(8,128)} %convolution_subtract_fusion.11), custom_call_target="Cholesky" | custom-call | tf_op jit(solution)/shard_map/jit(cholesky)/cholesky | solution.py:69
  253.3 10.6 %while.6 = (s32[]{:T(128)}, f32[384,384]{1,0:T(8,128)}, s32[3,2]{0,1:T(2,128)S(1)}, f32[3,128,128]{2,1,0:T(8,128)}, s32[]{:T(128)}) while((s32[]{:T(128)}, f32[384,384]{1,0:T(8,128)}, s32[3,2]{0,1:T(2,128)S(1)}, f32[3,128,128]{2,1,0:T(8,128)}, s32[]{:T(128)}) %tuple.72), condition=%wide.while_cond, body=%wide.while_body.sunk | while | flops 2 | bytes 132205 | solution.py:70
  254.0 2.9 bitcast_dynamic-update-slice_fusion.6
  257.5 2.9 bitcast_dynamic-update-slice_fusion.6
  261.1 2.8 bitcast_dynamic-update-slice_fusion.6
  263.9 31.3 %custom-call.25 = f32[3,128,128]{1,2,0:T(8,128)} custom-call(f32[3,128,128]{2,1,0:T(8,128)} %get-tuple-element.27), custom_call_target="InvertDiagBlocksLowerTriangular" | custom-call | tf_op jit(solution)/shard_map/triangular_solve/custom-call.2 | solution.py:70
  298.8 2.3 convolution_subtract_fusion.5
  301.7 7.5 %fusion.2 = f32[768,384]{1,0:T(8,128)S(1)} fusion(f32[768,768]{1,0:T(8,128)S(1)} %bitcast.182, f32[768,128]{0,1:T(8,128)S(1)} %fusion.58, f32[768,128]{0,1:T(8,128)S(1)} %fusion.59, f32[768,128]{0,1:T(8,128)S(1)} %bitcast.189), kind=kOutput, calls=%fused_computation.16 | convolution fusion | flops 2718498816 | bytes 4718592 | tf_op jit(solution)/shard_map/dot_general | solution.py:58
  309.2 4.0 fusion.125
  313.2 2.9 fusion.126
  321.0 13.2 %cholesky.326 = f32[128,128]{1,0:T(8,128)} custom-call(f32[128,128]{1,0:T(8,128)} %cholesky.436), custom_call_target="Cholesky" | custom-call | tf_op jit(solution)/shard_map/jit(cholesky)/cholesky | solution.py:69
  337.3 11.3 %custom-call.26 = f32[1,128,128]{1,2,0:T(8,128)} custom-call(f32[1,128,128]{2,1,0:T(8,128)} %get-tuple-element.75), custom_call_target="InvertDiagBlocksLowerTriangular" | custom-call | tf_op jit(solution)/shard_map/jit(cholesky)/cholesky | solution.py:69
  352.9 13.4 %cholesky.345 = f32[128,128]{1,0:T(8,128)} custom-call(f32[128,128]{1,0:T(8,128)} %cholesky.440), custom_call_target="Cholesky" | custom-call | tf_op jit(solution)/shard_map/jit(cholesky)/cholesky | solution.py:69
  367.7 11.3 %custom-call.27 = f32[1,128,128]{1,2,0:T(8,128)} custom-call(f32[1,128,128]{2,1,0:T(8,128)} %get-tuple-element.72), custom_call_target="InvertDiagBlocksLowerTriangular" | custom-call | tf_op jit(solution)/shard_map/jit(cholesky)/cholesky | solution.py:69
  382.6 13.2 %cholesky.364 = f32[128,128]{1,0:T(8,128)} custom-call(f32[128,128]{1,0:T(8,128)} %convolution_subtract_fusion.10), custom_call_target="Cholesky" | custom-call | tf_op jit(solution)/shard_map/jit(cholesky)/cholesky | solution.py:69
  403.8 10.6 %while.7 = (s32[]{:T(128)}, f32[384,384]{1,0:T(8,128)}, s32[3,2]{0,1:T(2,128)S(1)}, f32[3,128,128]{2,1,0:T(8,128)}, s32[]{:T(128)}) while((s32[]{:T(128)}, f32[384,384]{1,0:T(8,128)}, s32[3,2]{0,1:T(2,128)S(1)}, f32[3,128,128]{2,1,0:T(8,128)}, s32[]{:T(128)}) %tuple.85), condition=%wide.while_cond.clone, body=%wide.while_body.clone.sunk | while | flops 2 | bytes 132205 | solution.py:70
  404.4 2.9 bitcast_dynamic-update-slice_fusion.7
  408.0 2.9 bitcast_dynamic-update-slice_fusion.7
  411.5 2.8 bitcast_dynamic-update-slice_fusion.7
  414.3 31.3 %custom-call.28 = f32[3,128,128]{1,2,0:T(8,128)} custom-call(f32[3,128,128]{2,1,0:T(8,128)} %get-tuple-element.28), custom_call_target="InvertDiagBlocksLowerTriangular" | custom-call | tf_op jit(solution)/shard_map/triangular_solve/custom-call.2 | solution.py:70
  449.3 2.3 convolution_subtract_fusion.4
  452.1 7.5 %fusion.8 = f32[768,384]{1,0:T(8,128)S(1)} fusion(f32[768,768]{1,0:T(8,128)S(1)} %bitcast.184, f32[768,128]{0,1:T(8,128)S(1)} %fusion.53, f32[768,128]{0,1:T(8,128)S(1)} %fusion.54, f32[768,128]{0,1:T(8,128)S(1)} %bitcast.191), kind=kOutput, calls=%fused_computation.22 | convolution fusion | flops 2718498816 | bytes 4718592 | tf_op jit(solution)/shard_map/dot_general | solution.py:58
  459.6 4.0 fusion.127
  463.6 2.9 fusion.128
  471.4 13.2 %cholesky.379 = f32[128,128]{1,0:T(8,128)} custom-call(f32[128,128]{1,0:T(8,128)} %cholesky.444), custom_call_target="Cholesky" | custom-call | tf_op jit(solution)/shard_map/jit(cholesky)/cholesky | solution.py:69
  487.7 11.3 %custom-call.29 = f32[1,128,128]{1,2,0:T(8,128)} custom-call(f32[1,128,128]{2,1,0:T(8,128)} %get-tuple-element.68), custom_call_target="InvertDiagBlocksLowerTriangular" | custom-call | tf_op jit(solution)/shard_map/jit(cholesky)/cholesky | solution.py:69
  503.3 13.4 %cholesky.398 = f32[128,128]{1,0:T(8,128)} custom-call(f32[128,128]{1,0:T(8,128)} %cholesky.448), custom_call_target="Cholesky" | custom-call | tf_op jit(solution)/shard_map/jit(cholesky)/cholesky | solution.py:69
  518.1 11.3 %custom-call.30 = f32[1,128,128]{1,2,0:T(8,128)} custom-call(f32[1,128,128]{2,1,0:T(8,128)} %get-tuple-element.65), custom_call_target="InvertDiagBlocksLowerTriangular" | custom-call | tf_op jit(solution)/shard_map/jit(cholesky)/cholesky | solution.py:69
  533.0 13.2 %cholesky.417 = f32[128,128]{1,0:T(8,128)} custom-call(f32[128,128]{1,0:T(8,128)} %convolution_subtract_fusion.9), custom_call_target="Cholesky" | custom-call | tf_op jit(solution)/shard_map/jit(cholesky)/cholesky | solution.py:69
  554.2 10.6 %while.8 = (s32[]{:T(128)}, f32[384,384]{1,0:T(8,128)}, s32[3,2]{0,1:T(2,128)S(1)}, f32[3,128,128]{2,1,0:T(8,128)}, s32[]{:T(128)}) while((s32[]{:T(128)}, f32[384,384]{1,0:T(8,128)}, s32[3,2]{0,1:T(2,128)S(1)}, f32[3,128,128]{2,1,0:T(8,128)}, s32[]{:T(128)}) %tuple.86), condition=%wide.while_cond.clone.1, body=%wide.while_body.clone.1.sunk | while | flops 2 | bytes 132205 | solution.py:70
  554.8 2.9 bitcast_dynamic-update-slice_fusion.8
  558.4 2.9 bitcast_dynamic-update-slice_fusion.8
  561.9 2.8 bitcast_dynamic-update-slice_fusion.8
  564.7 31.1 %custom-call.31 = f32[3,128,128]{1,2,0:T(8,128)} custom-call(f32[3,128,128]{2,1,0:T(8,128)} %get-tuple-element.29), custom_call_target="InvertDiagBlocksLowerTriangular" | custom-call | tf_op jit(solution)/shard_map/triangular_solve/custom-call.2 | solution.py:70
  599.5 2.3 convolution_subtract_fusion.3
  604.3 3.2 collective-permute-start
  (122 shorter events, 101.8 us)
Async XLA Ops:
  6.5 68.6 %all-gather.3.cloned.1.call-start = ((), (), s32[]{:S(2)}) async-start(), calls=%async_computation | async-start | bytes 2506752 | tf_op jit(solution)/shard_map/all_gather | solution.py:80
  8.2 141.0 %all-gather.5.cloned.1.call-start = ((), (), s32[]{:S(2)}) async-start(), calls=%async_computation.1 | async-start | bytes 1216512 | tf_op jit(solution)/shard_map/all_gather | solution.py:86
  160.5 0.8 copy-start
  202.0 0.7 copy-start.3
  295.2 3.1 copy-start.6
  319.5 0.8 copy-start.1
  351.6 0.7 copy-start.4
  445.6 3.1 copy-start.7
  469.9 0.8 copy-start.2
  502.0 0.7 copy-start.5
  595.9 3.1 copy-start.8
  604.3 4.9 collective-permute-start
Sparse Core Ops, SparseCore 0:
  10.3 64.7 all-gather.2
  77.2 71.9 all-gather.4
where the time goes:
time: 630 us; the launch traced here: 619 us
  other arithmetic  320 us (51%)
  waiting for transfers between devices  109 us (17%)
  matrix products  98.8 us (16%)
  local copies, waits for them, and re-layouts  59.9 us (10%)
  between operations  28.1 us (4%)
    another operation x32, other arithmetic, orthonormal(): chol_factor = jnp.linalg.cholesky(gram_matrix)  215 us
    another operation x8, other arithmetic, orthonormal(): lax.linalg.triangular_solve(chol_factor, sketched, left_side=False, lower...  99.6 us
    all_gather x1, waiting for transfers between devices, on_device(): full_sketch = lax.all_gather(sketch, 'bond', axis=0, tiled=True)  56.2 us
    all_gather x1, waiting for transfers between devices, on_device(): both = lax.all_gather(both, 'row', axis=0, tiled=True)  51.3 us
    another operation x32, local copies, waits for them, and re-layouts, orthonormal(): lax.linalg.triangular_solve(chol_factor, sketched, left_side=False, lower...  34.2 us
    dot_general x6, matrix products, inner_rows(): lax.dot_general(left_side, right_side, (((0,), (0,)), ((), ())), precisio...  25.5 us
    another operation x12, matrix products, orthonormal(): chol_factor = jnp.linalg.cholesky(gram_matrix)  19.9 us
    another operation x15, matrix products, orthonormal(): lax.linalg.triangular_solve(chol_factor, sketched, left_side=False, lower...  19.2 us
  transfers between devices with their start and end apart: 3, of which 3 were waited for; matrix products, arithmetic and copies ran while one was open for 4% of the time, Pallas kernels for 0%

commit v1 on v0

--- a/solution.py
+++ b/solution.py
@@ -77,7 +77,24 @@
     local_sites = left_core.shape[1]
     local_rows = 2 * local_sites
     both = jnp.stack([left_core[0], right_core[0]], axis=1)
-    both = lax.all_gather(both, "row", axis=0, tiled=True)
+    size, index, rows = (lax.axis_size("row"), lax.axis_index("row"), both.shape[0])
+    right = [(i, (i + 1) % size) for i in range(size)]
+    left = [(i, (i - 1) % size) for i in range(size)]
+    result = jnp.zeros((*both.shape[:0], size * rows, *both.shape[0 + 1 :]), both.dtype)
+    result = lax.dynamic_update_slice_in_dim(result, both, index * rows, axis=0)
+    from_left = from_right = both
+    half = size // 2
+    for step in range(1, half + 1):
+        from_left = lax.ppermute(from_left, "row", right)
+        result = lax.dynamic_update_slice_in_dim(
+            result, from_left, (index - step) % size * rows, axis=0
+        )
+        if step < size - half:
+            from_right = lax.ppermute(from_right, "row", left)
+            result = lax.dynamic_update_slice_in_dim(
+                result, from_right, (index + step) % size * rows, axis=0
+            )
+    both = result
     sites = both.shape[0]
     left_matrix = both[:, 0].reshape(2 * sites, width)
     right_matrix = both[:, 1].reshape(sites, 2 * width)

time: 630 us -> 590 us (0.937)
  waiting for transfers between devices: 109 us -> 18.9 us
  starting transfers between devices: 3.24 us -> 72.8 us
  other arithmetic: 320 us -> 309 us
    ppermute x0 -> x15, starting transfers between devices: none -> 63.5 us  [the longest x7 46.1 us: on_device(): from_right = lax.ppermute(from_right, 'row', left)]
    all_gather x1, waiting for transfers between devices: 56.2 us -> 0.02 us  [on_device(): full_sketch = lax.all_gather(sketch, 'bond', axis=0, tiled=True)]
    all_gather x1 -> x0, waiting for transfers between devices: 51.3 us -> none  [on_device(): both = lax.all_gather(both, 'row', axis=0, tiled=True)]
    ppermute x0 -> x15, waiting for transfers between devices: none -> 12.6 us  [the longest x8 12.6 us: on_device(): from_left = lax.ppermute(from_left, 'row', right)]
    another operation x32, other arithmetic: 215 us -> 206 us  [orthonormal(): chol_factor = jnp.linalg.cholesky(gram_matrix)]
  transfers between devices with their start and end apart: 3 -> 17, of which waited for: 3 -> 8; matrix products, arithmetic and copies ran while one was open for 4% -> 3% of each run, Pallas kernels for 0% -> 0%
where the time goes in v1:
time: 590 us; the launch traced here: 584 us
  other arithmetic  309 us (52%)
  matrix products  94.4 us (16%)
  starting transfers between devices  72.8 us (12%)
  local copies, waits for them, and re-layouts  59.5 us (10%)
  between operations  28.7 us (5%)
  waiting for transfers between devices  18.9 us (3%)
    another operation x32, other arithmetic, orthonormal(): chol_factor = jnp.linalg.cholesky(gram_matrix)  206 us
    another operation x8, other arithmetic, orthonormal(): lax.linalg.triangular_solve(chol_factor, sketched, left_side=False, lower...  99 us
    ppermute x7, starting transfers between devices, on_device(): from_right = lax.ppermute(from_right, 'row', left)  46.1 us
    another operation x32, local copies, waits for them, and re-layouts, orthonormal(): lax.linalg.triangular_solve(chol_factor, sketched, left_side=False, lower...  34.6 us
    dot_general x6, matrix products, inner_rows(): lax.dot_general(left_side, right_side, (((0,), (0,)), ((), ())), precisio...  25.5 us
    another operation x12, matrix products, orthonormal(): chol_factor = jnp.linalg.cholesky(gram_matrix)  19.8 us
    another operation x15, matrix products, orthonormal(): lax.linalg.triangular_solve(chol_factor, sketched, left_side=False, lower...  19.2 us
    dot_general x5, matrix products, matmul(): jnp.dot(left_side, right_side, precision=HIGHEST, preferred_element_type=...  18.8 us
  transfers between devices with their start and end apart: 17, of which 8 were waited for; matrix products, arithmetic and copies ran while one was open for 3% of the time, Pallas kernels for 0%

profile of v1, /device:TPU:1, one launch (start us, length us, event | category | flops | bytes accessed | tf_op | source)
XLA Modules:
  0.0 583.6 jit_solution(11031836809452026607)
XLA Ops:
  7.6 3.9 collective-permute-start
  11.5 5.6 collective-permute-start.1
  29.3 6.7 %collective-permute-start.3 = (f32[24,2,2,384]{3,2,0,1:T(2,128)S(1)}, f32[24,2,2,384]{3,2,0,1:T(2,128)S(1)}, u32[]{:S(2)}, u32[]{:S(2)}) collective-permute-start(f32[24,2,2,384]{3,2,0,1:T(2,128)S(1)} %collective-permute-done.1), channel_id=1, source_target_pairs={{0,15},{1,0},{2,1},{3,2},{4,3},{5,4},{6,5},{7,6},{8,7},{9,8},{10,9... | collective-permute-start | bytes 442376 | tf_op jit(solution)/shard_map/ppermute | solution.py:93
  38.5 6.7 %collective-permute-start.5 = (f32[24,2,2,384]{3,2,0,1:T(2,128)S(1)}, f32[24,2,2,384]{3,2,0,1:T(2,128)S(1)}, u32[]{:S(2)}, u32[]{:S(2)}) collective-permute-start(f32[24,2,2,384]{3,2,0,1:T(2,128)S(1)} %collective-permute-done.3), channel_id=1, source_target_pairs={{0,15},{1,0},{2,1},{3,2},{4,3},{5,4},{6,5},{7,6},{8,7},{9,8},{10,9... | collective-permute-start | bytes 442376 | tf_op jit(solution)/shard_map/ppermute | solution.py:93
  47.6 6.7 %collective-permute-start.7 = (f32[24,2,2,384]{3,2,0,1:T(2,128)S(1)}, f32[24,2,2,384]{3,2,0,1:T(2,128)S(1)}, u32[]{:S(2)}, u32[]{:S(2)}) collective-permute-start(f32[24,2,2,384]{3,2,0,1:T(2,128)S(1)} %collective-permute-done.5), channel_id=1, source_target_pairs={{0,15},{1,0},{2,1},{3,2},{4,3},{5,4},{6,5},{7,6},{8,7},{9,8},{10,9... | collective-permute-start | bytes 442376 | tf_op jit(solution)/shard_map/ppermute | solution.py:93
  57.3 7.0 %collective-permute-start.9 = (f32[24,2,2,384]{3,2,0,1:T(2,128)S(1)}, f32[24,2,2,384]{3,2,0,1:T(2,128)S(1)}, u32[]{:S(2)}, u32[]{:S(2)}) collective-permute-start(f32[24,2,2,384]{3,2,0,1:T(2,128)S(1)} %collective-permute-done.7), channel_id=1, source_target_pairs={{0,15},{1,0},{2,1},{3,2},{4,3},{5,4},{6,5},{7,6},{8,7},{9,8},{10,9... | collective-permute-start | bytes 442376 | tf_op jit(solution)/shard_map/ppermute | solution.py:93
  68.3 6.7 %collective-permute-start.11 = (f32[24,2,2,384]{3,2,0,1:T(2,128)S(1)}, f32[24,2,2,384]{3,2,0,1:T(2,128)S(1)}, u32[]{:S(2)}, u32[]{:S(2)}) collective-permute-start(f32[24,2,2,384]{3,2,0,1:T(2,128)S(1)} %collective-permute-done.9), channel_id=1, source_target_pairs={{0,15},{1,0},{2,1},{3,2},{4,3},{5,4},{6,5},{7,6},{8,7},{9,8},{10,9... | collective-permute-start | bytes 442376 | tf_op jit(solution)/shard_map/ppermute | solution.py:93
  78.5 6.7 %collective-permute-start.13 = (f32[24,2,2,384]{3,2,0,1:T(2,128)S(1)}, f32[24,2,2,384]{3,2,0,1:T(2,128)S(1)}, u32[]{:S(2)}, u32[]{:S(2)}) collective-permute-start(f32[24,2,2,384]{3,2,0,1:T(2,128)S(1)} %collective-permute-done.11), channel_id=1, source_target_pairs={{0,15},{1,0},{2,1},{3,2},{4,3},{5,4},{6,5},{7,6},{8,7},{9,8},{10,9... | collective-permute-start | bytes 442376 | tf_op jit(solution)/shard_map/ppermute | solution.py:93
  88.0 7.0 %collective-permute-done.14 = f32[24,2,2,384]{3,2,0,1:T(2,128)S(1)} collective-permute-done((f32[24,2,2,384]{3,2,0,1:T(2,128)S(1)}, f32[24,2,2,384]{3,2,0,1:T(2,128)S(1)}, u32[]{:S(2)}, u32[]{:S(2)}) %collective-permute-start.14) | collective-permute-done | bytes 147488 | tf_op jit(solution)/shard_map/ppermute | solution.py:88
  96.6 4.1 convolution_bitcast_fusion
  100.7 10.3 %fusion = f32[384,384,2,2,1]{1,3,4,2,0:T(2,128)S(1)} fusion(f32[384,2,2,384,1]{3,0,2,1,4:T(8,128)S(1)} %convolution_bitcast_fusion, f32[2,2,2,2]{3,2,1,0:T(2,128)S(1)} %reshape.66), kind=kOutput, calls=%fused_computation.6 | convolution fusion | flops 28311552 | bytes 4718656 | tf_op jit(solution)/shard_map/pqtu,atuc->apqc/dot_general | solution.py:47
  111.2 5.1 fusion.123
  124.1 13.2 %cholesky.273 = f32[128,128]{1,0:T(8,128)} custom-call(f32[128,128]{1,0:T(8,128)} %cholesky.428), custom_call_target="Cholesky" | custom-call | tf_op jit(solution)/shard_map/jit(cholesky)/cholesky | solution.py:69
  140.4 11.7 %custom-call.23 = f32[1,128,128]{1,2,0:T(8,128)} custom-call(f32[1,128,128]{2,1,0:T(8,128)} %get-tuple-element.84), custom_call_target="InvertDiagBlocksLowerTriangular" | custom-call | tf_op jit(solution)/shard_map/jit(cholesky)/cholesky | solution.py:69
  156.4 13.2 %cholesky.292 = f32[128,128]{1,0:T(8,128)} custom-call(f32[128,128]{1,0:T(8,128)} %cholesky.432), custom_call_target="Cholesky" | custom-call | tf_op jit(solution)/shard_map/jit(cholesky)/cholesky | solution.py:69
  171.1 11.3 %custom-call.24 = f32[1,128,128]{1,2,0:T(8,128)} custom-call(f32[1,128,128]{2,1,0:T(8,128)} %get-tuple-element.81), custom_call_target="InvertDiagBlocksLowerTriangular" | custom-call | tf_op jit(solution)/shard_map/jit(cholesky)/cholesky | solution.py:69
  185.9 13.2 %cholesky.311 = f32[128,128]{1,0:T(8,128)} custom-call(f32[128,128]{1,0:T(8,128)} %convolution_subtract_fusion.11), custom_call_target="Cholesky" | custom-call | tf_op jit(solution)/shard_map/jit(cholesky)/cholesky | solution.py:69
  206.5 10.7 %while.6 = (s32[]{:T(128)}, f32[384,384]{1,0:T(8,128)}, s32[3,2]{0,1:T(2,128)S(1)}, f32[3,128,128]{2,1,0:T(8,128)}, s32[]{:T(128)}) while((s32[]{:T(128)}, f32[384,384]{1,0:T(8,128)}, s32[3,2]{0,1:T(2,128)S(1)}, f32[3,128,128]{2,1,0:T(8,128)}, s32[]{:T(128)}) %tuple.73), condition=%wide.while_cond, body=%wide.while_body.sunk | while | flops 2 | bytes 132205 | solution.py:70
  207.2 2.9 bitcast_dynamic-update-slice_fusion.6
  210.8 2.9 bitcast_dynamic-update-slice_fusion.6
  214.3 2.9 bitcast_dynamic-update-slice_fusion.6
  217.2 31.1 %custom-call.25 = f32[3,128,128]{1,2,0:T(8,128)} custom-call(f32[3,128,128]{2,1,0:T(8,128)} %get-tuple-element.27), custom_call_target="InvertDiagBlocksLowerTriangular" | custom-call | tf_op jit(solution)/shard_map/triangular_solve/custom-call.2 | solution.py:70
  254.8 7.5 %fusion.2 = f32[768,384]{1,0:T(8,128)S(1)} fusion(f32[768,768]{1,0:T(8,128)S(1)} %bitcast.182, f32[768,128]{0,1:T(8,128)S(1)} %fusion.58, f32[768,128]{0,1:T(8,128)S(1)} %fusion.59, f32[768,128]{0,1:T(8,128)S(1)} %bitcast.189), kind=kOutput, calls=%fused_computation.16 | convolution fusion | flops 2718498816 | bytes 4718592 | tf_op jit(solution)/shard_map/dot_general | solution.py:58
  262.3 4.1 fusion.125
  274.1 13.2 %cholesky.326 = f32[128,128]{1,0:T(8,128)} custom-call(f32[128,128]{1,0:T(8,128)} %cholesky.436), custom_call_target="Cholesky" | custom-call | tf_op jit(solution)/shard_map/jit(cholesky)/cholesky | solution.py:69
  290.4 11.3 %custom-call.26 = f32[1,128,128]{1,2,0:T(8,128)} custom-call(f32[1,128,128]{2,1,0:T(8,128)} %get-tuple-element.77), custom_call_target="InvertDiagBlocksLowerTriangular" | custom-call | tf_op jit(solution)/shard_map/jit(cholesky)/cholesky | solution.py:69
  306.0 13.6 %cholesky.345 = f32[128,128]{1,0:T(8,128)} custom-call(f32[128,128]{1,0:T(8,128)} %cholesky.440), custom_call_target="Cholesky" | custom-call | tf_op jit(solution)/shard_map/jit(cholesky)/cholesky | solution.py:69
  321.1 11.3 %custom-call.27 = f32[1,128,128]{1,2,0:T(8,128)} custom-call(f32[1,128,128]{2,1,0:T(8,128)} %get-tuple-element.74), custom_call_target="InvertDiagBlocksLowerTriangular" | custom-call | tf_op jit(solution)/shard_map/jit(cholesky)/cholesky | solution.py:69
  335.9 13.2 %cholesky.364 = f32[128,128]{1,0:T(8,128)} custom-call(f32[128,128]{1,0:T(8,128)} %convolution_subtract_fusion.10), custom_call_target="Cholesky" | custom-call | tf_op jit(solution)/shard_map/jit(cholesky)/cholesky | solution.py:69
  357.1 10.7 %while.7 = (s32[]{:T(128)}, f32[384,384]{1,0:T(8,128)}, s32[3,2]{0,1:T(2,128)S(1)}, f32[3,128,128]{2,1,0:T(8,128)}, s32[]{:T(128)}) while((s32[]{:T(128)}, f32[384,384]{1,0:T(8,128)}, s32[3,2]{0,1:T(2,128)S(1)}, f32[3,128,128]{2,1,0:T(8,128)}, s32[]{:T(128)}) %tuple.84), condition=%wide.while_cond.clone, body=%wide.while_body.clone.sunk | while | flops 2 | bytes 132205 | solution.py:70
  357.7 2.9 bitcast_dynamic-update-slice_fusion.7
  361.3 2.9 bitcast_dynamic-update-slice_fusion.7
  364.9 2.9 bitcast_dynamic-update-slice_fusion.7
  367.8 31.1 %custom-call.28 = f32[3,128,128]{1,2,0:T(8,128)} custom-call(f32[3,128,128]{2,1,0:T(8,128)} %get-tuple-element.28), custom_call_target="InvertDiagBlocksLowerTriangular" | custom-call | tf_op jit(solution)/shard_map/triangular_solve/custom-call.2 | solution.py:70
  405.3 7.5 %fusion.8 = f32[768,384]{1,0:T(8,128)S(1)} fusion(f32[768,768]{1,0:T(8,128)S(1)} %bitcast.184, f32[768,128]{0,1:T(8,128)S(1)} %fusion.53, f32[768,128]{0,1:T(8,128)S(1)} %fusion.54, f32[768,128]{0,1:T(8,128)S(1)} %bitcast.191), kind=kOutput, calls=%fused_computation.22 | convolution fusion | flops 2718498816 | bytes 4718592 | tf_op jit(solution)/shard_map/dot_general | solution.py:58
  412.9 4.1 fusion.127
  424.7 13.2 %cholesky.379 = f32[128,128]{1,0:T(8,128)} custom-call(f32[128,128]{1,0:T(8,128)} %cholesky.444), custom_call_target="Cholesky" | custom-call | tf_op jit(solution)/shard_map/jit(cholesky)/cholesky | solution.py:69
  441.0 11.3 %custom-call.29 = f32[1,128,128]{1,2,0:T(8,128)} custom-call(f32[1,128,128]{2,1,0:T(8,128)} %get-tuple-element.70), custom_call_target="InvertDiagBlocksLowerTriangular" | custom-call | tf_op jit(solution)/shard_map/jit(cholesky)/cholesky | solution.py:69
  456.6 13.6 %cholesky.398 = f32[128,128]{1,0:T(8,128)} custom-call(f32[128,128]{1,0:T(8,128)} %cholesky.448), custom_call_target="Cholesky" | custom-call | tf_op jit(solution)/shard_map/jit(cholesky)/cholesky | solution.py:69
  471.6 11.3 %custom-call.30 = f32[1,128,128]{1,2,0:T(8,128)} custom-call(f32[1,128,128]{2,1,0:T(8,128)} %get-tuple-element.67), custom_call_target="InvertDiagBlocksLowerTriangular" | custom-call | tf_op jit(solution)/shard_map/jit(cholesky)/cholesky | solution.py:69
  486.5 13.2 %cholesky.417 = f32[128,128]{1,0:T(8,128)} custom-call(f32[128,128]{1,0:T(8,128)} %convolution_subtract_fusion.9), custom_call_target="Cholesky" | custom-call | tf_op jit(solution)/shard_map/jit(cholesky)/cholesky | solution.py:69
  507.7 10.7 %while.8 = (s32[]{:T(128)}, f32[384,384]{1,0:T(8,128)}, s32[3,2]{0,1:T(2,128)S(1)}, f32[3,128,128]{2,1,0:T(8,128)}, s32[]{:T(128)}) while((s32[]{:T(128)}, f32[384,384]{1,0:T(8,128)}, s32[3,2]{0,1:T(2,128)S(1)}, f32[3,128,128]{2,1,0:T(8,128)}, s32[]{:T(128)}) %tuple.85), condition=%wide.while_cond.clone.1, body=%wide.while_body.clone.1.sunk | while | flops 2 | bytes 132205 | solution.py:70
  508.3 2.9 bitcast_dynamic-update-slice_fusion.8
  511.9 2.9 bitcast_dynamic-update-slice_fusion.8
  515.5 2.9 bitcast_dynamic-update-slice_fusion.8
  518.4 31.1 %custom-call.31 = f32[3,128,128]{1,2,0:T(8,128)} custom-call(f32[3,128,128]{2,1,0:T(8,128)} %get-tuple-element.29), custom_call_target="InvertDiagBlocksLowerTriangular" | custom-call | tf_op jit(solution)/shard_map/triangular_solve/custom-call.2 | solution.py:70
  557.9 9.3 %collective-permute-start.15 = (f32[24,768]{1,0:T(8,128)}, f32[24,768]{1,0:T(8,128)}, u32[]{:S(2)}, u32[]{:S(2)}) collective-permute-start(f32[24,768]{1,0:T(8,128)} %fusion.46), channel_id=1, source_target_pairs={{0,16},{16,32},{32,48},{48,64},{64,80},{80,96},{96,112},{112,128},... | collective-permute-start | bytes 221192 | tf_op jit(solution)/shard_map/ppermute | solution.py:15
  567.9 6.2 %collective-permute-done.15 = f32[24,768]{1,0:T(8,128)} collective-permute-done((f32[24,768]{1,0:T(8,128)}, f32[24,768]{1,0:T(8,128)}, u32[]{:S(2)}, u32[]{:S(2)}) %collective-permute-start.15) | collective-permute-done | bytes 73760 | tf_op jit(solution)/shard_map/ppermute | solution.py:15
  (195 shorter events, 132.9 us)
Async XLA Ops:
  6.5 104.7 %all-gather.2.cloned.1.call-start = ((), (), s32[]{:S(2)}) async-start(), calls=%async_computation | async-start | bytes 1216512 | tf_op jit(solution)/shard_map/all_gather | solution.py:103
  6.5 0.9 copy-start.9
  6.5 0.9 copy-start.10
  6.5 10.6 %copy-start.11 = (f32[1,6]{1,0:T(1,128)S(1)}, f32[1,6]{1,0:T(1,128)}, u32[]{:S(2)}) copy-start(f32[1,6]{1,0:T(1,128)} %param.27) | copy-start | bytes 76
  6.5 19.6 %copy-start.16 = (f32[4,4]{1,0:T(4,128)S(1)}, f32[4,4]{1,0:T(4,128)}, u32[]{:S(2)}) copy-start(f32[4,4]{1,0:T(4,128)} %constant.213.clone) | copy-start | bytes 196
  6.6 19.6 %copy-start.17 = (f32[4,4]{1,0:T(4,128)S(1)}, f32[4,4]{1,0:T(4,128)}, u32[]{:S(2)}) copy-start(f32[4,4]{1,0:T(4,128)} %constant.214.clone) | copy-start | bytes 196
  6.6 19.6 %copy-start.23 = (f32[4,4]{1,0:T(4,128)S(1)}, f32[4,4]{1,0:T(4,128)}, u32[]{:S(2)}) copy-start(f32[4,4]{1,0:T(4,128)} %constant.215.clone) | copy-start | bytes 196
  6.6 19.7 %copy-start.22 = (f32[4,4]{1,0:T(4,128)S(1)}, f32[4,4]{1,0:T(4,128)}, u32[]{:S(2)}) copy-start(f32[4,4]{1,0:T(4,128)} %constant.216.clone) | copy-start | bytes 196
  6.6 19.9 %copy-start.14 = (f32[4,4]{1,0:T(4,128)S(1)}, f32[4,4]{1,0:T(4,128)}, u32[]{:S(2)}) copy-start(f32[4,4]{1,0:T(4,128)} %constant.217.clone) | copy-start | bytes 196
  6.6 19.9 %copy-start.15 = (f32[4,4]{1,0:T(4,128)S(1)}, f32[4,4]{1,0:T(4,128)}, u32[]{:S(2)}) copy-start(f32[4,4]{1,0:T(4,128)} %constant.218.clone) | copy-start | bytes 196
  6.6 19.9 %copy-start.21 = (f32[4,4]{1,0:T(4,128)S(1)}, f32[4,4]{1,0:T(4,128)}, u32[]{:S(2)}) copy-start(f32[4,4]{1,0:T(4,128)} %constant.219.clone) | copy-start | bytes 196
  6.6 20.0 %copy-start.20 = (f32[4,4]{1,0:T(4,128)S(1)}, f32[4,4]{1,0:T(4,128)}, u32[]{:S(2)}) copy-start(f32[4,4]{1,0:T(4,128)} %constant.220.clone) | copy-start | bytes 196
  6.6 20.1 %copy-start.12 = (f32[4,4]{1,0:T(4,128)S(1)}, f32[4,4]{1,0:T(4,128)}, u32[]{:S(2)}) copy-start(f32[4,4]{1,0:T(4,128)} %constant.221.clone) | copy-start | bytes 196
  6.7 20.1 %copy-start.13 = (f32[4,4]{1,0:T(4,128)S(1)}, f32[4,4]{1,0:T(4,128)}, u32[]{:S(2)}) copy-start(f32[4,4]{1,0:T(4,128)} %constant.222.clone) | copy-start | bytes 196
  6.7 20.1 %copy-start.19 = (f32[4,4]{1,0:T(4,128)S(1)}, f32[4,4]{1,0:T(4,128)}, u32[]{:S(2)}) copy-start(f32[4,4]{1,0:T(4,128)} %constant.223.clone) | copy-start | bytes 196
  6.7 20.2 %copy-start.18 = (f32[4,4]{1,0:T(4,128)S(1)}, f32[4,4]{1,0:T(4,128)}, u32[]{:S(2)}) copy-start(f32[4,4]{1,0:T(4,128)} %constant.224.clone) | copy-start | bytes 196
  7.6 19.7 %collective-permute-start = (f32[24,2,2,384]{3,2,0,1:T(2,128)S(1)}, f32[24,2,2,384]{3,2,0,1:T(2,128)S(1)}, u32[]{:S(2)}, u32[]{:S(2)}) collective-permute-start(f32[24,2,2,384]{3,2,0,1:T(2,128)S(1)} %get-tuple-element.62), channel_id=1, source_target_pairs={{0,1},{1,2},{2,3},{3,4},{4,5},{5,6},{6,7},{7,8},{8,9},{9,10},{10,1... | collective-permute-start | bytes 442376 | tf_op jit(solution)/shard_map/ppermute | solution.py:88
  11.5 17.7 %collective-permute-start.1 = (f32[24,2,2,384]{3,2,0,1:T(2,128)S(1)}, f32[24,2,2,384]{3,2,0,1:T(2,128)S(1)}, u32[]{:S(2)}, u32[]{:S(2)}) collective-permute-start(f32[24,2,2,384]{3,2,0,1:T(2,128)S(1)} %get-tuple-element.62), channel_id=1, source_target_pairs={{0,15},{1,0},{2,1},{3,2},{4,3},{5,4},{6,5},{7,6},{8,7},{9,8},{10,9... | collective-permute-start | bytes 442376 | tf_op jit(solution)/shard_map/ppermute | solution.py:93
  27.3 9.2 %collective-permute-start.2 = (f32[24,2,2,384]{3,2,0,1:T(2,128)S(1)}, f32[24,2,2,384]{3,2,0,1:T(2,128)S(1)}, u32[]{:S(2)}, u32[]{:S(2)}) collective-permute-start(f32[24,2,2,384]{3,2,0,1:T(2,128)S(1)} %collective-permute-done), channel_id=1, source_target_pairs={{0,1},{1,2},{2,3},{3,4},{4,5},{5,6},{6,7},{7,8},{8,9},{9,10},{10,1... | collective-permute-start | bytes 442376 | tf_op jit(solution)/shard_map/ppermute | solution.py:88
  29.3 9.2 %collective-permute-start.3 = (f32[24,2,2,384]{3,2,0,1:T(2,128)S(1)}, f32[24,2,2,384]{3,2,0,1:T(2,128)S(1)}, u32[]{:S(2)}, u32[]{:S(2)}) collective-permute-start(f32[24,2,2,384]{3,2,0,1:T(2,128)S(1)} %collective-permute-done.1), channel_id=1, source_target_pairs={{0,15},{1,0},{2,1},{3,2},{4,3},{5,4},{6,5},{7,6},{8,7},{9,8},{10,9... | collective-permute-start | bytes 442376 | tf_op jit(solution)/shard_map/ppermute | solution.py:93
  36.5 9.2 %collective-permute-start.4 = (f32[24,2,2,384]{3,2,0,1:T(2,128)S(1)}, f32[24,2,2,384]{3,2,0,1:T(2,128)S(1)}, u32[]{:S(2)}, u32[]{:S(2)}) collective-permute-start(f32[24,2,2,384]{3,2,0,1:T(2,128)S(1)} %collective-permute-done.2), channel_id=1, source_target_pairs={{0,1},{1,2},{2,3},{3,4},{4,5},{5,6},{6,7},{7,8},{8,9},{9,10},{10,1... | collective-permute-start | bytes 442376 | tf_op jit(solution)/shard_map/ppermute | solution.py:88
  38.5 9.2 %collective-permute-start.5 = (f32[24,2,2,384]{3,2,0,1:T(2,128)S(1)}, f32[24,2,2,384]{3,2,0,1:T(2,128)S(1)}, u32[]{:S(2)}, u32[]{:S(2)}) collective-permute-start(f32[24,2,2,384]{3,2,0,1:T(2,128)S(1)} %collective-permute-done.3), channel_id=1, source_target_pairs={{0,15},{1,0},{2,1},{3,2},{4,3},{5,4},{6,5},{7,6},{8,7},{9,8},{10,9... | collective-permute-start | bytes 442376 | tf_op jit(solution)/shard_map/ppermute | solution.py:93
  45.7 9.6 %collective-permute-start.6 = (f32[24,2,2,384]{3,2,0,1:T(2,128)S(1)}, f32[24,2,2,384]{3,2,0,1:T(2,128)S(1)}, u32[]{:S(2)}, u32[]{:S(2)}) collective-permute-start(f32[24,2,2,384]{3,2,0,1:T(2,128)S(1)} %collective-permute-done.4), channel_id=1, source_target_pairs={{0,1},{1,2},{2,3},{3,4},{4,5},{5,6},{6,7},{7,8},{8,9},{9,10},{10,1... | collective-permute-start | bytes 442376 | tf_op jit(solution)/shard_map/ppermute | solution.py:88
  47.6 9.6 %collective-permute-start.7 = (f32[24,2,2,384]{3,2,0,1:T(2,128)S(1)}, f32[24,2,2,384]{3,2,0,1:T(2,128)S(1)}, u32[]{:S(2)}, u32[]{:S(2)}) collective-permute-start(f32[24,2,2,384]{3,2,0,1:T(2,128)S(1)} %collective-permute-done.5), channel_id=1, source_target_pairs={{0,15},{1,0},{2,1},{3,2},{4,3},{5,4},{6,5},{7,6},{8,7},{9,8},{10,9... | collective-permute-start | bytes 442376 | tf_op jit(solution)/shard_map/ppermute | solution.py:93
  55.3 11.0 %collective-permute-start.8 = (f32[24,2,2,384]{3,2,0,1:T(2,128)S(1)}, f32[24,2,2,384]{3,2,0,1:T(2,128)S(1)}, u32[]{:S(2)}, u32[]{:S(2)}) collective-permute-start(f32[24,2,2,384]{3,2,0,1:T(2,128)S(1)} %collective-permute-done.6), channel_id=1, source_target_pairs={{0,1},{1,2},{2,3},{3,4},{4,5},{5,6},{6,7},{7,8},{8,9},{9,10},{10,1... | collective-permute-start | bytes 442376 | tf_op jit(solution)/shard_map/ppermute | solution.py:88
  57.3 11.0 %collective-permute-start.9 = (f32[24,2,2,384]{3,2,0,1:T(2,128)S(1)}, f32[24,2,2,384]{3,2,0,1:T(2,128)S(1)}, u32[]{:S(2)}, u32[]{:S(2)}) collective-permute-start(f32[24,2,2,384]{3,2,0,1:T(2,128)S(1)} %collective-permute-done.7), channel_id=1, source_target_pairs={{0,15},{1,0},{2,1},{3,2},{4,3},{5,4},{6,5},{7,6},{8,7},{9,8},{10,9... | collective-permute-start | bytes 442376 | tf_op jit(solution)/shard_map/ppermute | solution.py:93
  66.4 10.2 %collective-permute-start.10 = (f32[24,2,2,384]{3,2,0,1:T(2,128)S(1)}, f32[24,2,2,384]{3,2,0,1:T(2,128)S(1)}, u32[]{:S(2)}, u32[]{:S(2)}) collective-permute-start(f32[24,2,2,384]{3,2,0,1:T(2,128)S(1)} %collective-permute-done.8), channel_id=1, source_target_pairs={{0,1},{1,2},{2,3},{3,4},{4,5},{5,6},{6,7},{7,8},{8,9},{9,10},{10,1... | collective-permute-start | bytes 442376 | tf_op jit(solution)/shard_map/ppermute | solution.py:88
  68.3 10.2 %collective-permute-start.11 = (f32[24,2,2,384]{3,2,0,1:T(2,128)S(1)}, f32[24,2,2,384]{3,2,0,1:T(2,128)S(1)}, u32[]{:S(2)}, u32[]{:S(2)}) collective-permute-start(f32[24,2,2,384]{3,2,0,1:T(2,128)S(1)} %collective-permute-done.9), channel_id=1, source_target_pairs={{0,15},{1,0},{2,1},{3,2},{4,3},{5,4},{6,5},{7,6},{8,7},{9,8},{10,9... | collective-permute-start | bytes 442376 | tf_op jit(solution)/shard_map/ppermute | solution.py:93
  76.6 9.2 %collective-permute-start.12 = (f32[24,2,2,384]{3,2,0,1:T(2,128)S(1)}, f32[24,2,2,384]{3,2,0,1:T(2,128)S(1)}, u32[]{:S(2)}, u32[]{:S(2)}) collective-permute-start(f32[24,2,2,384]{3,2,0,1:T(2,128)S(1)} %collective-permute-done.10), channel_id=1, source_target_pairs={{0,1},{1,2},{2,3},{3,4},{4,5},{5,6},{6,7},{7,8},{8,9},{9,10},{10,1... | collective-permute-start | bytes 442376 | tf_op jit(solution)/shard_map/ppermute | solution.py:88
  78.5 9.4 %collective-permute-start.13 = (f32[24,2,2,384]{3,2,0,1:T(2,128)S(1)}, f32[24,2,2,384]{3,2,0,1:T(2,128)S(1)}, u32[]{:S(2)}, u32[]{:S(2)}) collective-permute-start(f32[24,2,2,384]{3,2,0,1:T(2,128)S(1)} %collective-permute-done.11), channel_id=1, source_target_pairs={{0,15},{1,0},{2,1},{3,2},{4,3},{5,4},{6,5},{7,6},{8,7},{9,8},{10,9... | collective-permute-start | bytes 442376 | tf_op jit(solution)/shard_map/ppermute | solution.py:93
  85.8 9.2 %collective-permute-start.14 = (f32[24,2,2,384]{3,2,0,1:T(2,128)S(1)}, f32[24,2,2,384]{3,2,0,1:T(2,128)S(1)}, u32[]{:S(2)}, u32[]{:S(2)}) collective-permute-start(f32[24,2,2,384]{3,2,0,1:T(2,128)S(1)} %collective-permute-done.12), channel_id=1, source_target_pairs={{0,1},{1,2},{2,3},{3,4},{4,5},{5,6},{6,7},{7,8},{8,9},{9,10},{10,1... | collective-permute-start | bytes 442376 | tf_op jit(solution)/shard_map/ppermute | solution.py:88
  122.6 0.8 copy-start
  155.1 0.7 copy-start.3
  248.3 3.1 copy-start.6
  272.6 0.8 copy-start.1
  304.7 0.7 copy-start.4
  398.9 3.1 copy-start.7
  423.2 0.8 copy-start.2
  455.3 0.7 copy-start.5
  549.5 3.1 copy-start.8
  557.9 16.3 %collective-permute-start.15 = (f32[24,768]{1,0:T(8,128)}, f32[24,768]{1,0:T(8,128)}, u32[]{:S(2)}, u32[]{:S(2)}) collective-permute-start(f32[24,768]{1,0:T(8,128)} %fusion.46), channel_id=1, source_target_pairs={{0,16},{16,32},{32,48},{48,64},{64,80},{80,96},{96,112},{112,128},... | collective-permute-start | bytes 221192 | tf_op jit(solution)/shard_map/ppermute | solution.py:15
Sparse Core Ops, SparseCore 0:
  17.3 72.5 all-gather.1
